TPU v7x, 32 devices: a whole 2x2x4 slice. The times are simulated.
32 devices in a mesh: gz: 4 (over x, core), gy: 4 (over z), gx: 2 (over y).
Axes of the slice: x: 2, y: 2, z: 4, core: 2. Of those that a mesh axis runs over, the one named last changes fastest.
Arguments:
- volume: bfloat16 [32, 4, 32, 384], P('gz', 'gy', 'gx'), may hold values from -80 to 80
- cotangent: bfloat16 [32, 4, 32, 384], P('gz', 'gy', 'gx'), may hold values from -6 to 6
- w_project: bfloat16 [3, 384, 1152], P(None, 'gy', ('gz', 'gx')), may hold values from -0.3125 to 0.3125
- w_output: bfloat16 [3, 384, 384], P(None, 'gy', ('gz', 'gx')), may hold values from -0.3125 to 0.3125
Outputs:
- grad_volume: bfloat16 [32, 4, 32, 384], P('gz', 'gy', 'gx')
All inputs are finite; a program needn't handle non-finite values.
Results may differ from a plain program's by a relative error of at most 0.015.
Values may be sent and summed in bfloat16 or wider, within the bound.
No kernel may reach another device: no remote copies, remote signals or barrier semaphores. Data moves between devices by JAX's collectives and lax.ppermute only.
A program may use at most 64 MiB of HBM per device.

v0:
```python
import jax
import jax.numpy as jnp
from jax import lax
from jax.sharding import PartitionSpec as P

HEADS = 6


def head_norm(vector):
    return (vector * lax.rsqrt(jnp.mean(vector * vector, axis=-1, keepdims=True) + 1e-06)).astype(
        jnp.bfloat16
    )


def sublayer(line_rows, w_inner, w_outer):
    feat_len = line_rows.shape[-1]
    head_size = feat_len // HEADS
    stream = line_rows.astype(jnp.float32)
    normed = (stream * lax.rsqrt(jnp.mean(stream * stream, axis=-1, keepdims=True) + 1e-06)).astype(
        jnp.bfloat16
    )
    packed = jnp.dot(normed, w_inner, preferred_element_type=jnp.float32)
    head_shape = line_rows.shape[:3] + (HEADS, head_size)
    queries = head_norm(packed[..., :feat_len].reshape(head_shape))
    key_part = head_norm(packed[..., feat_len : 2 * feat_len].reshape(head_shape))
    value_part = packed[..., 2 * feat_len :].reshape(head_shape).astype(jnp.bfloat16)
    scores = jnp.einsum(
        "plqhe,pkqhe->pqhlk", queries, key_part, preferred_element_type=jnp.float32
    ) * head_size ** (-0.5)
    powers = jnp.exp(scores)
    attn_weights = (powers / jnp.sum(powers, axis=-1, keepdims=True)).astype(jnp.bfloat16)
    mixed_out = jnp.einsum(
        "pqhlk,pkqhe->plqhe", attn_weights, value_part, preferred_element_type=jnp.float32
    )
    mixed_out = mixed_out.astype(jnp.bfloat16).reshape(line_rows.shape)
    update = jnp.dot(mixed_out, w_outer, preferred_element_type=jnp.float32)
    return (stream + update).astype(jnp.bfloat16)


def along_depth(member, w_inner, w_outer):
    depth_len, row_len, rest_len, feat_len = member.shape
    flat_lines = member.reshape(1, depth_len, row_len * rest_len, feat_len)
    return sublayer(flat_lines, w_inner, w_outer).reshape(member.shape)


def along_rows(member, w_inner, w_outer):
    return sublayer(member, w_inner, w_outer)


def along_columns(member, w_inner, w_outer):
    depth_len, row_len, col_len, feat_len = member.shape
    flat_lines = member.reshape(depth_len * row_len, col_len, 1, feat_len)
    return sublayer(flat_lines, w_inner, w_outer).reshape(member.shape)


def backward_pass(local_fn, activ_lines, grad_lines):
    _, pullback = jax.vjp(local_fn, activ_lines)
    return pullback(grad_lines)[0]


def depth_out(stacked):
    return lax.all_to_all(stacked, "gz", split_axis=3, concat_axis=1, tiled=True)


def depth_in(stacked):
    return lax.all_to_all(stacked, "gz", split_axis=1, concat_axis=3, tiled=True)


def rows_out(stacked):
    return lax.all_to_all(stacked, "gy", split_axis=3, concat_axis=2, tiled=True)


def rows_in(stacked):
    return lax.all_to_all(stacked, "gy", split_axis=2, concat_axis=3, tiled=True)


def columns_out(stacked):
    return lax.all_to_all(stacked, "gx", split_axis=1, concat_axis=3, tiled=True)


def columns_in(stacked):
    return lax.all_to_all(stacked, "gx", split_axis=3, concat_axis=1, tiled=True)


def local(volume, cotangent, w_project, w_output):
    part_proj, part_outp = (
        lax.all_gather(w_project, "gy", axis=1, tiled=True),
        lax.all_gather(w_output, "gy", axis=1, tiled=True),
    )
    proj_full, outp_full = (
        lax.all_gather(part_proj, ("gz", "gx"), axis=2, tiled=True),
        lax.all_gather(part_outp, ("gz", "gx"), axis=2, tiled=True),
    )

    def depth_fn(member):
        return along_depth(member, proj_full[0], outp_full[0])

    def row_fn(member):
        return along_rows(member, proj_full[1], outp_full[1])

    def column_fn(member):
        return along_columns(member, proj_full[2], outp_full[2])

    depth_act = depth_out(volume[None])[0]
    field_one = depth_in(depth_fn(depth_act)[None])[0]
    row_act = rows_out(field_one[None])[0]
    field_two = rows_in(row_fn(row_act)[None])[0]
    paired = columns_out(jnp.stack([cotangent, field_two]))
    grad_two = columns_in(backward_pass(column_fn, paired[1], paired[0])[None])[0]
    row_grad = rows_out(grad_two[None])[0]
    grad_one = rows_in(backward_pass(row_fn, row_act, row_grad)[None])[0]
    depth_grad = depth_out(grad_one[None])[0]
    grad_zero = depth_in(backward_pass(depth_fn, depth_act, depth_grad)[None])[0]
    return grad_zero


def solution(mesh):
    return jax.shard_map(
        local,
        mesh=mesh,
        in_specs=(
            P("gz", "gy", "gx", None),
            P("gz", "gy", "gx", None),
            P(None, "gy", ("gz", "gx")),
            P(None, "gy", ("gz", "gx")),
        ),
        out_specs=P("gz", "gy", "gx", None),
        check_vma=False,
    )
```

profile of v0, /device:TPU:0, one launch (start us, length us, event | category | flops | bytes accessed | tf_op | source)
XLA Modules:
  0.0 244.8 jit_solution(7430313849005049411)
XLA Ops:
  7.6 21.3 %all_gather.12 = bf16[3,384,144]{2,0,1:T(4,128)(2,1)S(1)} all-gather(bf16[3,96,144]{2,0,1:T(4,128)(2,1)S(1)} %copy.364), channel_id=1, replica_groups=mesh['gz'=4,'gy'=4,'gx'=2] {'gy'}, dimensions={1}, use_global_device_ids=true | all-gather | bytes 414720 | tf_op jit(solution)/shard_map/all_gather | solution.py:87
  31.0 3.3 %all-to-all-start = ((bf16[1,8,1,16,384]{4,1,2,0,3:T(8,128)(2,1)}), bf16[1,8,1,16,384]{4,1,2,0,3:T(8,128)(2,1)S(1)}, u32[]{:S(2)}, u32[]{:S(2)}) async-start(bf16[1,8,1,16,384]{4,1,2,0,3:T(8,128)(2,1)} %bitcast.315), calls=%async_computation | async-start | bytes 196608 | tf_op jit(solution)/shard_map/all_to_all | solution.py:62
  34.4 15.0 %all_gather.14 = bf16[3,384,48]{2,0,1:T(4,128)(2,1)S(1)} all-gather(bf16[3,96,48]{2,0,1:T(4,128)(2,1)S(1)} %copy.376), channel_id=1, replica_groups=mesh['gz'=4,'gy'=4,'gx'=2] {'gy'}, dimensions={1}, use_global_device_ids=true | all-gather | bytes 138240 | tf_op jit(solution)/shard_map/all_gather | solution.py:88
  49.7 20.0 %all_gather.15 = bf16[3,384,384]{1,2,0:T(8,128)(2,1)S(1)} all-gather(bf16[3,384,48]{1,2,0:T(8,128)(2,1)S(1)} %copy.377), channel_id=1, replica_groups=mesh['gz'=4,'gy'=4,'gx'=2] {'gz','gx'}, dimensions={2}, use_global_device_ids=true | all-gather | bytes 995328 | tf_op jit(solution)/shard_map/all_gather | solution.py:92
  76.5 7.0 %all_to_all.132 = bf16[1,32,1,4,384]{4,3,2,0,1:T(4,128)(2,1)S(1)} all-to-all(bf16[1,32,1,4,384]{4,3,2,0,1:T(4,128)(2,1)S(1)} %copy.379), channel_id=1, replica_groups=mesh['gz'=4,'gy'=4,'gx'=2] {'gz'}, dimensions={1} | all-to-all | bytes 196608 | tf_op jit(solution)/shard_map/all_to_all | solution.py:66
  83.6 8.7 %all_to_all.133 = bf16[1,8,1,16,384]{4,1,2,0,3:T(8,128)(2,1)S(1)} all-to-all(bf16[1,8,1,16,384]{4,1,2,0,3:T(8,128)(2,1)S(1)} %bitcast.338), channel_id=1, replica_groups=mesh['gz'=4,'gy'=4,'gx'=2] {'gy'}, dimensions={3} | all-to-all | bytes 196608 | tf_op jit(solution)/shard_map/all_to_all | solution.py:70
  102.1 8.2 %all_to_all.134 = bf16[1,8,4,4,384]{4,1,3,0,2:T(8,128)(2,1)S(1)} all-to-all(bf16[1,8,4,4,384]{4,1,3,0,2:T(8,128)(2,1)S(1)} %fusion.28), channel_id=1, replica_groups=mesh['gz'=4,'gy'=4,'gx'=2] {'gy'}, dimensions={2} | all-to-all | bytes 196608 | tf_op jit(solution)/shard_map/all_to_all | solution.py:74
  111.2 7.2 %all_to_all.135 = bf16[2,8,1,16,384]{4,3,2,0,1:T(8,128)(2,1)S(1)} all-to-all(bf16[2,8,1,16,384]{4,3,2,0,1:T(8,128)(2,1)S(1)} %pad_maximum_fusion), channel_id=1, replica_groups=mesh['gz'=4,'gy'=4,'gx'=2] {'gx'}, dimensions={1} | all-to-all | bytes 393216 | tf_op jit(solution)/shard_map/all_to_all | solution.py:78
  126.6 1.9 reshape.731
  128.5 1.8 reshape.734
  130.3 1.9 multiply_reduce_fusion
  145.8 1.9 fusion.21
  158.7 1.8 reshape.736
  162.9 1.9 multiply_reduce_fusion.14
  166.0 6.7 %all_to_all.136 = bf16[1,4,1,32,384]{4,1,2,0,3:T(4,128)(2,1)S(1)} all-to-all(bf16[1,4,1,32,384]{4,1,2,0,3:T(4,128)(2,1)S(1)} %copy.424), channel_id=1, replica_groups=mesh['gz'=4,'gy'=4,'gx'=2] {'gx'}, dimensions={3} | all-to-all | bytes 196608 | tf_op jit(solution)/shard_map/all_to_all | solution.py:82
  174.9 3.9 %all-to-all-start.6 = ((bf16[1,8,1,16,384]{4,1,2,0,3:T(8,128)(2,1)}), bf16[1,8,1,16,384]{4,1,2,0,3:T(8,128)(2,1)}, u32[]{:S(2)}, u32[]{:S(2)}) async-start(bf16[1,8,1,16,384]{4,1,2,0,3:T(8,128)(2,1)} %all_to_all.112), calls=%async_computation.6 | async-start | bytes 196608 | tf_op jit(solution)/shard_map/all_to_all | solution.py:70
  179.5 5.2 %all-to-all-done.6 = bf16[1,8,1,16,384]{4,1,2,0,3:T(8,128)(2,1)} async-done(((bf16[1,8,1,16,384]{4,1,2,0,3:T(8,128)(2,1)}), bf16[1,8,1,16,384]{4,1,2,0,3:T(8,128)(2,1)}, u32[]{:S(2)}, u32[]{:S(2)}) %all-to-all-start.6) | async-done | bytes 98336 | tf_op jit(solution)/shard_map/all_to_all | solution.py:70
  188.2 2.1 fusion.14
  199.2 2.0 add_add_fusion.2
  208.0 3.9 %all-to-all-start.7 = ((bf16[1,8,4,4,384]{4,1,3,0,2:T(8,128)(2,1)}), bf16[1,8,4,4,384]{4,1,3,0,2:T(8,128)(2,1)}, u32[]{:S(2)}, u32[]{:S(2)}) async-start(bf16[1,8,4,4,384]{4,1,3,0,2:T(8,128)(2,1)} %fusion.88), calls=%async_computation.7 | async-start | bytes 196608 | tf_op jit(solution)/shard_map/all_to_all | solution.py:74
  212.1 5.8 %all-to-all-done.7 = bf16[1,8,4,4,384]{4,1,3,0,2:T(8,128)(2,1)} async-done(((bf16[1,8,4,4,384]{4,1,3,0,2:T(8,128)(2,1)}), bf16[1,8,4,4,384]{4,1,3,0,2:T(8,128)(2,1)}, u32[]{:S(2)}, u32[]{:S(2)}) %all-to-all-start.7) | async-done | bytes 98336 | tf_op jit(solution)/shard_map/all_to_all | solution.py:74
  217.9 3.5 %all-to-all-start.8 = ((bf16[1,8,1,16,384]{4,1,2,0,3:T(8,128)(2,1)}), bf16[1,8,1,16,384]{4,1,2,0,3:T(8,128)(2,1)S(1)}, u32[]{:S(2)}, u32[]{:S(2)}) async-start(bf16[1,8,1,16,384]{4,1,2,0,3:T(8,128)(2,1)} %bitcast.68), calls=%async_computation.8 | async-start | bytes 196608 | tf_op jit(solution)/shard_map/all_to_all | solution.py:62
  221.5 4.0 %all-to-all-done.8 = bf16[1,8,1,16,384]{4,1,2,0,3:T(8,128)(2,1)S(1)} async-done(((bf16[1,8,1,16,384]{4,1,2,0,3:T(8,128)(2,1)}), bf16[1,8,1,16,384]{4,1,2,0,3:T(8,128)(2,1)S(1)}, u32[]{:S(2)}, u32[]{:S(2)}) %all-to-all-start.8) | async-done | bytes 98336 | tf_op jit(solution)/shard_map/all_to_all | solution.py:62
  230.6 6.7 %all_to_all.137 = bf16[1,32,1,4,384]{4,3,2,0,1:T(4,128)(2,1)S(1)} all-to-all(bf16[1,32,1,4,384]{4,3,2,0,1:T(4,128)(2,1)S(1)} %copy.469), channel_id=1, replica_groups=mesh['gz'=4,'gy'=4,'gx'=2] {'gz'}, dimensions={1} | all-to-all | bytes 196608 | tf_op jit(solution)/shard_map/all_to_all | solution.py:66
  (253 shorter events, 84.6 us)
Async XLA Ops:
  6.5 23.8 %copy-start.38 = (bf16[8,1,16,384]{3,2,1,0:T(8,128)(2,1)S(1)}, bf16[8,1,16,384]{3,2,1,0:T(8,128)(2,1)}, u32[]{:S(2)}) copy-start(bf16[8,1,16,384]{3,2,1,0:T(8,128)(2,1)} %param.4) | copy-start | bytes 294916
  6.5 27.8 %copy-start.42 = (bf16[3,96,48]{1,2,0:T(8,128)(2,1)S(1)}, bf16[3,96,48]{1,2,0:T(8,128)(2,1)}, u32[]{:S(2)}) copy-start(bf16[3,96,48]{1,2,0:T(8,128)(2,1)} %param.7) | copy-start | bytes 82948
  6.5 63.9 %all-gather.2.cloned.1.call-start = ((), (), s32[]{:S(2)}) async-start(), calls=%async_computation.10 | async-start | bytes 2985984 | tf_op jit(solution)/shard_map/all_gather | solution.py:91
  31.0 38.7 %all-to-all-start = ((bf16[1,8,1,16,384]{4,1,2,0,3:T(8,128)(2,1)}), bf16[1,8,1,16,384]{4,1,2,0,3:T(8,128)(2,1)S(1)}, u32[]{:S(2)}, u32[]{:S(2)}) async-start(bf16[1,8,1,16,384]{4,1,2,0,3:T(8,128)(2,1)} %bitcast.315), calls=%async_computation | async-start | bytes 196608 | tf_op jit(solution)/shard_map/all_to_all | solution.py:62
  69.7 6.5 %copy-start.1 = (bf16[1,8,1,16,384]{4,1,2,0,3:T(8,128)(2,1)}, bf16[1,8,1,16,384]{4,1,2,0,3:T(8,128)(2,1)S(1)}, u32[]{:S(2)}) copy-start(bf16[1,8,1,16,384]{4,1,2,0,3:T(8,128)(2,1)S(1)} %all-to-all-done) | copy-start | bytes 294916
  74.9 19.8 %copy-start.40 = (f32[4,6,32]{2,1,0:T(8,128)}, f32[4,6,32]{2,1,0:T(8,128)S(1)}, u32[]{:S(2)}) copy-start(f32[4,6,32]{2,1,0:T(8,128)S(1)} %get-tuple-element.25) | copy-start | bytes 9220
  92.3 9.5 %copy-start.3 = (bf16[1,8,1,16,384]{4,1,2,0,3:T(8,128)(2,1)}, bf16[1,8,1,16,384]{4,1,2,0,3:T(8,128)(2,1)S(1)}, u32[]{:S(2)}) copy-start(bf16[1,8,1,16,384]{4,1,2,0,3:T(8,128)(2,1)S(1)} %all_to_all.133) | copy-start | bytes 294916
  95.0 5.9 %copy-start.26 = (bf16[8,4,4,6,64]{4,3,0,2,1:T(8,128)(2,1)}, bf16[8,4,4,6,64]{4,3,0,2,1:T(8,128)(2,1)S(1)}, u32[]{:S(2)}) copy-start(bf16[8,4,4,6,64]{4,3,0,2,1:T(8,128)(2,1)S(1)} %convert_element_type.384) | copy-start | bytes 294916
  147.9 6.9 %copy-start.37 = (f32[4,32,6]{1,0,2:T(4,128)S(1)}, f32[4,32,6]{1,0,2:T(4,128)}, u32[]{:S(2)}) copy-start(f32[4,32,6]{1,0,2:T(4,128)} %copy.401) | copy-start | bytes 9220
  162.9 15.9 %copy-start.10 = (f32[8,4,6,4]{3,2,1,0:T(8,128)S(1)}, f32[8,4,6,4]{3,2,1,0:T(8,128)}, u32[]{:S(2)}) copy-start(f32[8,4,6,4]{3,2,1,0:T(8,128)} %copy-done.9) | copy-start | bytes 9220
  162.9 27.4 %copy-start.6 = (f32[8,4,6,4,4]{3,4,2,1,0:T(4,128)S(1)}, f32[8,4,6,4,4]{3,4,2,1,0:T(4,128)}, u32[]{:S(2)}) copy-start(f32[8,4,6,4,4]{3,4,2,1,0:T(4,128)} %copy-done.5) | copy-start | bytes 36868
  174.9 9.8 %all-to-all-start.6 = ((bf16[1,8,1,16,384]{4,1,2,0,3:T(8,128)(2,1)}), bf16[1,8,1,16,384]{4,1,2,0,3:T(8,128)(2,1)}, u32[]{:S(2)}, u32[]{:S(2)}) async-start(bf16[1,8,1,16,384]{4,1,2,0,3:T(8,128)(2,1)} %all_to_all.112), calls=%async_computation.6 | async-start | bytes 196608 | tf_op jit(solution)/shard_map/all_to_all | solution.py:70
  188.2 5.1 %copy-start.29 = (bf16[8,4,4,6,64]{4,0,3,2,1:T(8,128)(2,1)S(1)}, bf16[8,4,4,6,64]{4,0,3,2,1:T(8,128)(2,1)}, u32[]{:S(2)}) copy-start(bf16[8,4,4,6,64]{4,0,3,2,1:T(8,128)(2,1)} %copy-done.28) | copy-start | bytes 294916
  192.2 6.8 %copy-start.23 = (f32[8,4,4,6]{3,0,2,1:T(8,128)S(1)}, f32[8,4,4,6]{3,0,2,1:T(8,128)}, u32[]{:S(2)}) copy-start(f32[8,4,4,6]{3,0,2,1:T(8,128)} %copy-done.22) | copy-start | bytes 9220
  192.2 7.0 %copy-start.21 = (f32[8,4,4,6]{0,3,2,1:T(8,128)S(1)}, f32[8,4,4,6]{0,3,2,1:T(8,128)}, u32[]{:S(2)}) copy-start(f32[8,4,4,6]{0,3,2,1:T(8,128)} %copy-done.20) | copy-start | bytes 9220
  199.2 5.4 %copy-start.4 = (bf16[1,8,1,16,384]{4,1,2,0,3:T(8,128)(2,1)S(1)}, bf16[1,8,1,16,384]{4,1,2,0,3:T(8,128)(2,1)}, u32[]{:S(2)}) copy-start(bf16[1,8,1,16,384]{4,1,2,0,3:T(8,128)(2,1)} %copy-done.3) | copy-start | bytes 294916
  203.5 8.5 %copy-start.43 = (f32[4,8,4]{1,0,2:T(4,128)S(1)}, f32[4,8,4]{1,0,2:T(4,128)}, u32[]{:S(2)}) copy-start(f32[4,8,4]{1,0,2:T(4,128)} %get-tuple-element.13) | copy-start | bytes 1540
  203.5 17.9 %copy-start.41 = (f32[4,6,32]{2,1,0:T(8,128)S(1)}, f32[4,6,32]{2,1,0:T(8,128)}, u32[]{:S(2)}) copy-start(f32[4,6,32]{2,1,0:T(8,128)} %copy-done.40) | copy-start | bytes 9220
  203.5 17.9 %copy-start.32 = (f32[32,4,6]{0,1,2:T(4,128)S(1)}, f32[32,4,6]{0,1,2:T(4,128)}, u32[]{:S(2)}) copy-start(f32[32,4,6]{0,1,2:T(4,128)} %copy-done.31) | copy-start | bytes 9220
  204.4 21.5 %copy-start.8 = (f32[4,6,32,32]{2,3,1,0:T(8,128)S(1)}, f32[4,6,32,32]{2,3,1,0:T(8,128)}, u32[]{:S(2)}) copy-start(f32[4,6,32,32]{2,3,1,0:T(8,128)} %copy-done.7) | copy-start | bytes 294916
  204.6 21.5 %copy-start.12 = (bf16[32,4,6,64]{3,2,0,1:T(8,128)(2,1)S(1)}, bf16[32,4,6,64]{3,2,0,1:T(8,128)(2,1)}, u32[]{:S(2)}) copy-start(bf16[32,4,6,64]{3,2,0,1:T(8,128)(2,1)} %copy-done.11) | copy-start | bytes 294916
  206.3 20.0 %copy-start.18 = (bf16[32,4,6,64]{3,2,0,1:T(8,128)(2,1)S(1)}, bf16[32,4,6,64]{3,2,0,1:T(8,128)(2,1)}, u32[]{:S(2)}) copy-start(bf16[32,4,6,64]{3,2,0,1:T(8,128)(2,1)} %copy-done.17) | copy-start | bytes 294916
  208.0 9.8 %all-to-all-start.7 = ((bf16[1,8,4,4,384]{4,1,3,0,2:T(8,128)(2,1)}), bf16[1,8,4,4,384]{4,1,3,0,2:T(8,128)(2,1)}, u32[]{:S(2)}, u32[]{:S(2)}) async-start(bf16[1,8,4,4,384]{4,1,3,0,2:T(8,128)(2,1)} %fusion.88), calls=%async_computation.7 | async-start | bytes 196608 | tf_op jit(solution)/shard_map/all_to_all | solution.py:74
  217.9 7.6 %all-to-all-start.8 = ((bf16[1,8,1,16,384]{4,1,2,0,3:T(8,128)(2,1)}), bf16[1,8,1,16,384]{4,1,2,0,3:T(8,128)(2,1)S(1)}, u32[]{:S(2)}, u32[]{:S(2)}) async-start(bf16[1,8,1,16,384]{4,1,2,0,3:T(8,128)(2,1)} %bitcast.68), calls=%async_computation.8 | async-start | bytes 196608 | tf_op jit(solution)/shard_map/all_to_all | solution.py:62
  (26 other events, 52.6 us)
Sparse Core Ops, SparseCore 0:
  30.4 30.7 all-gather.1
where the time goes:
time: 247 us; the launch traced here: 245 us
  blocking collectives  101 us (41%)
  local copies, waits for them, and re-layouts  45.4 us (18%)
  matrix products  28.5 us (12%)
  other arithmetic  25.9 us (10%)
  waiting for transfers between devices  15 us (6%)
  starting transfers between devices  14.7 us (6%)
  between operations  14.6 us (6%)
    all_gather x1, blocking collectives, local(): lax.all_gather(w_project, 'gy', axis=1, tiled=True)  21.3 us
    all_gather x1, blocking collectives, local(): lax.all_gather(part_outp, ('gz', 'gx'), axis=2, tiled=True)  20 us
    all_gather x1, blocking collectives, local(): lax.all_gather(w_output, 'gy', axis=1, tiled=True)  15 us
    all_to_all x2, blocking collectives, depth_in(): lax.all_to_all(stacked, 'gz', split_axis=1, concat_axis=3, tiled=True)  13.7 us
    dot_general x6, matrix products, sublayer(): packed = jnp.dot(normed, w_inner, preferred_element_type=jnp.float32)  9.92 us
    all_to_all x1, blocking collectives, rows_out(): lax.all_to_all(stacked, 'gy', split_axis=3, concat_axis=2, tiled=True)  8.69 us
    all_to_all x1, blocking collectives, rows_in(): lax.all_to_all(stacked, 'gy', split_axis=2, concat_axis=3, tiled=True)  8.21 us
    dot_general x9, matrix products, sublayer(): jnp.einsum('plqhe,pkqhe->pqhlk', queries, key_part, preferred_element_typ...  7.53 us
  transfers between devices with their start and end apart: 5, of which 3 were waited for; matrix products, arithmetic and copies ran while one was open for 1% of the time, Pallas kernels for 0%

commit v1 on v0

--- a/solution.py
+++ b/solution.py
@@ -1,9 +1,41 @@
+import functools
 import jax
 import jax.numpy as jnp
 from jax import lax
 from jax.sharding import PartitionSpec as P
 
 HEADS = 6
+
+
+def point_lane_now(vec, net_axis, ndim_at):
+    known, k_now, piece_next = (
+        jax.lax.axis_size(net_axis),
+        jax.lax.axis_index(net_axis),
+        vec.shape[ndim_at],
+    )
+    tile_out = lax.dynamic_update_slice_in_dim(
+        jnp.zeros([m * known if i0 == ndim_at else m for i0, m in enumerate(vec.shape)], vec.dtype),
+        vec,
+        k_now * piece_next,
+        axis=ndim_at,
+    )
+    fresh = taken_in = vec
+    for ix in range(1, known // 2 + 1):
+        fresh = jax.lax.ppermute(fresh, net_axis, [(i0, (i0 + 1) % known) for i0 in range(known)])
+        tile_out = lax.dynamic_update_slice_in_dim(
+            tile_out, fresh, (k_now - ix) % known * piece_next, axis=ndim_at
+        )
+        if 2 * ix < known:
+            taken_in = jax.lax.ppermute(
+                taken_in, net_axis, [(i0, (i0 - 1) % known) for i0 in range(known)]
+            )
+            tile_out = lax.dynamic_update_slice_in_dim(
+                tile_out, taken_in, (k_now + ix) % known * piece_next, axis=ndim_at
+            )
+    return tile_out
+
+
+obtain_block = functools.partial(point_lane_now, net_axis=("gz", "gx"), ndim_at=2)
 
 
 def head_norm(vector):
@@ -89,7 +121,7 @@
     )
     proj_full, outp_full = (
         lax.all_gather(part_proj, ("gz", "gx"), axis=2, tiled=True),
-        lax.all_gather(part_outp, ("gz", "gx"), axis=2, tiled=True),
+        obtain_block(part_outp),
     )
 
     def depth_fn(member):

time: 247 us -> 289 us (1.17)
  local copies, waits for them, and re-layouts: 45.4 us -> 69.4 us
  waiting for transfers between devices: 15 us -> 38.9 us
  blocking collectives: 101 us -> 82.9 us
  starting transfers between devices: 14.7 us -> 26.6 us
    dynamic_update_slice x0 -> x8, local copies, waits for them, and re-layouts: none -> 24.1 us  [the longest x4 12.3 us: point_lane_now(): lax.dynamic_update_slice_in_dim(tile_out, fresh, (k_now - ix) % known * p...]
    ppermute x0 -> x7, waiting for transfers between devices: none -> 23.9 us  [the longest x4 13 us: point_lane_now(): jax.lax.ppermute(fresh, net_axis, [(i0, (i0 + 1) % known) for i0 in range...]
    all_gather x1 -> x0, blocking collectives: 20 us -> none  [local(): lax.all_gather(part_outp, ('gz', 'gx'), axis=2, tiled=True)]
    ppermute x0 -> x7, starting transfers between devices: none -> 11.6 us  [the longest x4 9 us: point_lane_now(): jax.lax.ppermute(fresh, net_axis, [(i0, (i0 + 1) % known) for i0 in range...]
  transfers between devices with their start and end apart: 5 -> 12, of which waited for: 3 -> 6; matrix products, arithmetic and copies ran while one was open for 1% -> 9% of each run, Pallas kernels for 0% -> 0%
where the time goes in v1:
time: 289 us; the launch traced here: 287 us
  blocking collectives  82.9 us (29%)
  local copies, waits for them, and re-layouts  69.4 us (24%)
  waiting for transfers between devices  38.9 us (13%)
  matrix products  28.5 us (10%)
  starting transfers between devices  26.6 us (9%)
  other arithmetic  25.8 us (9%)
  between operations  14.6 us (5%)
    all_gather x1, blocking collectives, local(): lax.all_gather(w_project, 'gy', axis=1, tiled=True)  21.3 us
    all_to_all x2, blocking collectives, depth_in(): lax.all_to_all(stacked, 'gz', split_axis=1, concat_axis=3, tiled=True)  16.3 us
    all_gather x1, blocking collectives, local(): lax.all_gather(w_output, 'gy', axis=1, tiled=True)  14.5 us
    ppermute x4, waiting for transfers between devices, point_lane_now(): jax.lax.ppermute(fresh, net_axis, [(i0, (i0 + 1) % known) for i0 in range...  13 us
    dynamic_update_slice x4, local copies, waits for them, and re-layouts, point_lane_now(): lax.dynamic_update_slice_in_dim(tile_out, fresh, (k_now - ix) % known * p...  12.3 us
    ppermute x3, waiting for transfers between devices, point_lane_now(): jax.lax.ppermute(taken_in, net_axis, [(i0, (i0 - 1) % known) for i0 in ra...  10.8 us
    dot_general x6, matrix products, sublayer(): packed = jnp.dot(normed, w_inner, preferred_element_type=jnp.float32)  9.92 us
    dynamic_update_slice x3, local copies, waits for them, and re-layouts, point_lane_now(): lax.dynamic_update_slice_in_dim(tile_out, taken_in, (k_now + ix) % known...  9.59 us
  transfers between devices with their start and end apart: 12, of which 6 were waited for; matrix products, arithmetic and copies ran while one was open for 9% of the time, Pallas kernels for 0%

profile of v1, /device:TPU:0, one launch (start us, length us, event | category | flops | bytes accessed | tf_op | source)
XLA Modules:
  0.0 286.8 jit_solution(10362774706944139564)
XLA Ops:
  7.6 21.3 %all_gather.9 = bf16[3,384,144]{2,0,1:T(4,128)(2,1)S(1)} all-gather(bf16[3,96,144]{2,0,1:T(4,128)(2,1)S(1)} %copy.356), channel_id=1, replica_groups=mesh['gz'=4,'gy'=4,'gx'=2] {'gy'}, dimensions={1}, use_global_device_ids=true | all-gather | bytes 414720 | tf_op jit(solution)/shard_map/all_gather | solution.py:119
  30.4 14.5 %all_gather.11 = bf16[3,384,48]{2,1,0:T(8,128)(2,1)S(1)} all-gather(bf16[3,96,48]{2,1,0:T(8,128)(2,1)S(1)} %copy.368), channel_id=1, replica_groups=mesh['gz'=4,'gy'=4,'gx'=2] {'gy'}, dimensions={1}, use_global_device_ids=true | all-gather | bytes 138240 | tf_op jit(solution)/shard_map/all_gather | solution.py:120
  47.6 13.0 %collective-permute-done = bf16[3,384,48]{2,1,0:T(8,128)(2,1)S(1)} collective-permute-done((bf16[3,384,48]{2,1,0:T(8,128)(2,1)S(1)}, bf16[3,384,48]{2,1,0:T(8,128)(2,1)S(1)}, u32[]{:S(2)}, u32[]{:S(2)}) %collective-permute-start) | collective-permute-done | bytes 110624 | tf_op jit(solution)/shard_map/ppermute | solution.py:24
  63.8 3.7 %all-to-all-start = ((bf16[1,8,1,16,384]{4,1,2,0,3:T(8,128)(2,1)}), bf16[1,8,1,16,384]{4,1,2,0,3:T(8,128)(2,1)S(1)}, u32[]{:S(2)}, u32[]{:S(2)}) async-start(bf16[1,8,1,16,384]{4,1,2,0,3:T(8,128)(2,1)} %bitcast.310), calls=%async_computation | async-start | bytes 196608 | tf_op jit(solution)/shard_map/all_to_all | solution.py:94
  73.9 9.6 %collective-permute-done.3 = bf16[3,384,48]{2,1,0:T(8,128)(2,1)S(1)} collective-permute-done((bf16[3,384,48]{2,1,0:T(8,128)(2,1)S(1)}, bf16[3,384,48]{2,1,0:T(8,128)(2,1)S(1)}, u32[]{:S(2)}, u32[]{:S(2)}) %collective-permute-start.3) | collective-permute-done | bytes 110624 | tf_op jit(solution)/shard_map/ppermute | solution.py:29
  83.5 3.6 %collective-permute-start.6 = (bf16[3,384,48]{2,1,0:T(8,128)(2,1)S(1)}, bf16[3,384,48]{2,1,0:T(8,128)(2,1)S(1)}, u32[]{:S(2)}, u32[]{:S(2)}) collective-permute-start(bf16[3,384,48]{2,1,0:T(8,128)(2,1)S(1)} %collective-permute-done.4), channel_id=1, source_target_pairs={{0,1},{1,8},{8,9},{9,16},{16,17},{17,24},{24,25},{25,0},{2,3},{3,1... | collective-permute-start | bytes 331784 | tf_op jit(solution)/shard_map/ppermute | solution.py:24
  90.6 3.2 %dynamic_update_slice.26 = bf16[3,384,384]{2,1,0:T(8,128)(2,1)S(1)} dynamic-update-slice(bf16[3,384,384]{2,1,0:T(8,128)(2,1)S(1)} %dynamic_update_slice.25, bf16[3,384,48]{2,1,0:T(8,128)(2,1)S(1)} %collective-permute-done.1, s32[]{:T(128)} %constant.103.clone.1, s32[]{:T(128)} %constant.103.clone.1, s32[]{:T(128)S(6)} %select_n.59) | dynamic-update-slice | bytes 221188 | tf_op jit(solution)/shard_map/dynamic_update_slice | solution.py:32
  93.8 3.0 %dynamic_update_slice.27 = bf16[3,384,384]{2,1,0:T(8,128)(2,1)S(1)} dynamic-update-slice(bf16[3,384,384]{2,1,0:T(8,128)(2,1)S(1)} %dynamic_update_slice.26, bf16[3,384,48]{2,1,0:T(8,128)(2,1)S(1)} %collective-permute-done.2, s32[]{:T(128)} %constant.103.clone.1, s32[]{:T(128)} %constant.103.clone.1, s32[]{:T(128)S(6)} %select_n.61) | dynamic-update-slice | bytes 221188 | tf_op jit(solution)/shard_map/dynamic_update_slice | solution.py:25
  96.8 3.2 %dynamic_update_slice.28 = bf16[3,384,384]{2,1,0:T(8,128)(2,1)S(1)} dynamic-update-slice(bf16[3,384,384]{2,1,0:T(8,128)(2,1)S(1)} %dynamic_update_slice.27, bf16[3,384,48]{2,1,0:T(8,128)(2,1)S(1)} %collective-permute-done.3, s32[]{:T(128)} %constant.103.clone.1, s32[]{:T(128)} %constant.103.clone.1, s32[]{:T(128)S(6)} %select_n.63) | dynamic-update-slice | bytes 221188 | tf_op jit(solution)/shard_map/dynamic_update_slice | solution.py:32
  100.0 3.2 %dynamic_update_slice.29 = bf16[3,384,384]{2,1,0:T(8,128)(2,1)S(1)} dynamic-update-slice(bf16[3,384,384]{2,1,0:T(8,128)(2,1)S(1)} %dynamic_update_slice.28, bf16[3,384,48]{2,1,0:T(8,128)(2,1)S(1)} %collective-permute-done.4, s32[]{:T(128)} %constant.103.clone.1, s32[]{:T(128)} %constant.103.clone.1, s32[]{:T(128)S(6)} %select_n.65) | dynamic-update-slice | bytes 221188 | tf_op jit(solution)/shard_map/dynamic_update_slice | solution.py:25
  103.2 3.2 %dynamic_update_slice.30 = bf16[3,384,384]{2,1,0:T(8,128)(2,1)S(1)} dynamic-update-slice(bf16[3,384,384]{2,1,0:T(8,128)(2,1)S(1)} %dynamic_update_slice.29, bf16[3,384,48]{2,1,0:T(8,128)(2,1)S(1)} %collective-permute-done.5, s32[]{:T(128)} %constant.103.clone.1, s32[]{:T(128)} %constant.103.clone.1, s32[]{:T(128)S(6)} %select_n.67) | dynamic-update-slice | bytes 221188 | tf_op jit(solution)/shard_map/dynamic_update_slice | solution.py:32
  106.4 3.2 %dynamic_update_slice.31 = bf16[3,384,384]{2,1,0:T(8,128)(2,1)S(1)} dynamic-update-slice(bf16[3,384,384]{2,1,0:T(8,128)(2,1)S(1)} %dynamic_update_slice.30, bf16[3,384,48]{2,1,0:T(8,128)(2,1)S(1)} %collective-permute-done.6, s32[]{:T(128)} %constant.103.clone.1, s32[]{:T(128)} %constant.103.clone.1, s32[]{:T(128)S(6)} %select_n.69) | dynamic-update-slice | bytes 221188 | tf_op jit(solution)/shard_map/dynamic_update_slice | solution.py:25
  115.8 9.7 %all_to_all.132 = bf16[1,32,1,4,384]{4,3,2,0,1:T(4,128)(2,1)S(1)} all-to-all(bf16[1,32,1,4,384]{4,3,2,0,1:T(4,128)(2,1)S(1)} %copy.369), channel_id=1, replica_groups=mesh['gz'=4,'gy'=4,'gx'=2] {'gz'}, dimensions={1} | all-to-all | bytes 196608 | tf_op jit(solution)/shard_map/all_to_all | solution.py:98
  125.5 8.2 %all_to_all.133 = bf16[1,8,1,16,384]{4,1,2,0,3:T(8,128)(2,1)S(1)} all-to-all(bf16[1,8,1,16,384]{4,1,2,0,3:T(8,128)(2,1)S(1)} %bitcast.333), channel_id=1, replica_groups=mesh['gz'=4,'gy'=4,'gx'=2] {'gy'}, dimensions={3} | all-to-all | bytes 196608 | tf_op jit(solution)/shard_map/all_to_all | solution.py:102
  143.5 8.2 %all_to_all.134 = bf16[1,8,4,4,384]{4,1,3,0,2:T(8,128)(2,1)S(1)} all-to-all(bf16[1,8,4,4,384]{4,1,3,0,2:T(8,128)(2,1)S(1)} %fusion.28), channel_id=1, replica_groups=mesh['gz'=4,'gy'=4,'gx'=2] {'gy'}, dimensions={2} | all-to-all | bytes 196608 | tf_op jit(solution)/shard_map/all_to_all | solution.py:106
  152.6 7.7 %all_to_all.135 = bf16[2,8,1,16,384]{4,3,2,0,1:T(8,128)(2,1)S(1)} all-to-all(bf16[2,8,1,16,384]{4,3,2,0,1:T(8,128)(2,1)S(1)} %pad_maximum_fusion), channel_id=1, replica_groups=mesh['gz'=4,'gy'=4,'gx'=2] {'gx'}, dimensions={1} | all-to-all | bytes 393216 | tf_op jit(solution)/shard_map/all_to_all | solution.py:110
  207.9 6.7 %all_to_all.136 = bf16[1,4,1,32,384]{4,1,2,0,3:T(4,128)(2,1)S(1)} all-to-all(bf16[1,4,1,32,384]{4,1,2,0,3:T(4,128)(2,1)S(1)} %copy.412), channel_id=1, replica_groups=mesh['gz'=4,'gy'=4,'gx'=2] {'gx'}, dimensions={3} | all-to-all | bytes 196608 | tf_op jit(solution)/shard_map/all_to_all | solution.py:114
  216.7 4.2 %all-to-all-start.6 = ((bf16[1,8,1,16,384]{4,1,2,0,3:T(8,128)(2,1)}), bf16[1,8,1,16,384]{4,1,2,0,3:T(8,128)(2,1)}, u32[]{:S(2)}, u32[]{:S(2)}) async-start(bf16[1,8,1,16,384]{4,1,2,0,3:T(8,128)(2,1)} %all_to_all.112), calls=%async_computation.6 | async-start | bytes 196608 | tf_op jit(solution)/shard_map/all_to_all | solution.py:102
  221.6 5.0 %all-to-all-done.6 = bf16[1,8,1,16,384]{4,1,2,0,3:T(8,128)(2,1)} async-done(((bf16[1,8,1,16,384]{4,1,2,0,3:T(8,128)(2,1)}), bf16[1,8,1,16,384]{4,1,2,0,3:T(8,128)(2,1)}, u32[]{:S(2)}, u32[]{:S(2)}) %all-to-all-start.6) | async-done | bytes 98336 | tf_op jit(solution)/shard_map/all_to_all | solution.py:102
  250.0 3.9 %all-to-all-start.7 = ((bf16[1,8,4,4,384]{4,1,3,0,2:T(8,128)(2,1)}), bf16[1,8,4,4,384]{4,1,3,0,2:T(8,128)(2,1)}, u32[]{:S(2)}, u32[]{:S(2)}) async-start(bf16[1,8,4,4,384]{4,1,3,0,2:T(8,128)(2,1)} %fusion.88), calls=%async_computation.7 | async-start | bytes 196608 | tf_op jit(solution)/shard_map/all_to_all | solution.py:106
  254.0 5.8 %all-to-all-done.7 = bf16[1,8,4,4,384]{4,1,3,0,2:T(8,128)(2,1)} async-done(((bf16[1,8,4,4,384]{4,1,3,0,2:T(8,128)(2,1)}), bf16[1,8,4,4,384]{4,1,3,0,2:T(8,128)(2,1)}, u32[]{:S(2)}, u32[]{:S(2)}) %all-to-all-start.7) | async-done | bytes 98336 | tf_op jit(solution)/shard_map/all_to_all | solution.py:106
  259.8 3.3 %all-to-all-start.8 = ((bf16[1,8,1,16,384]{4,1,2,0,3:T(8,128)(2,1)}), bf16[1,8,1,16,384]{4,1,2,0,3:T(8,128)(2,1)S(1)}, u32[]{:S(2)}, u32[]{:S(2)}) async-start(bf16[1,8,1,16,384]{4,1,2,0,3:T(8,128)(2,1)} %bitcast.68), calls=%async_computation.8 | async-start | bytes 196608 | tf_op jit(solution)/shard_map/all_to_all | solution.py:94
  263.2 4.2 %all-to-all-done.8 = bf16[1,8,1,16,384]{4,1,2,0,3:T(8,128)(2,1)S(1)} async-done(((bf16[1,8,1,16,384]{4,1,2,0,3:T(8,128)(2,1)}), bf16[1,8,1,16,384]{4,1,2,0,3:T(8,128)(2,1)S(1)}, u32[]{:S(2)}, u32[]{:S(2)}) %all-to-all-start.8) | async-done | bytes 98336 | tf_op jit(solution)/shard_map/all_to_all | solution.py:94
  272.6 6.7 %all_to_all.137 = bf16[1,32,1,4,384]{4,3,2,0,1:T(4,128)(2,1)S(1)} all-to-all(bf16[1,32,1,4,384]{4,3,2,0,1:T(4,128)(2,1)S(1)} %copy.457), channel_id=1, replica_groups=mesh['gz'=4,'gy'=4,'gx'=2] {'gz'}, dimensions={1} | all-to-all | bytes 196608 | tf_op jit(solution)/shard_map/all_to_all | solution.py:98
  (274 shorter events, 114.1 us)
Async XLA Ops:
  6.5 23.8 %copy-start.42 = (bf16[3,96,48]{1,2,0:T(8,128)(2,1)S(1)}, bf16[3,96,48]{1,2,0:T(8,128)(2,1)}, u32[]{:S(2)}) copy-start(bf16[3,96,48]{1,2,0:T(8,128)(2,1)} %param.7) | copy-start | bytes 82948
  6.5 56.6 %copy-start.38 = (bf16[8,1,16,384]{3,2,1,0:T(8,128)(2,1)S(1)}, bf16[8,1,16,384]{3,2,1,0:T(8,128)(2,1)}, u32[]{:S(2)}) copy-start(bf16[8,1,16,384]{3,2,1,0:T(8,128)(2,1)} %param.4) | copy-start | bytes 294916
  6.5 103.1 %all-gather.2.cloned.1.call-start = ((), (), s32[]{:S(2)}) async-start(), calls=%async_computation.10 | async-start | bytes 2985984 | tf_op jit(solution)/shard_map/all_gather | solution.py:123
  44.9 15.7 %collective-permute-start = (bf16[3,384,48]{2,1,0:T(8,128)(2,1)S(1)}, bf16[3,384,48]{2,1,0:T(8,128)(2,1)S(1)}, u32[]{:S(2)}, u32[]{:S(2)}) collective-permute-start(bf16[3,384,48]{2,1,0:T(8,128)(2,1)S(1)} %all_gather.11), channel_id=1, source_target_pairs={{0,1},{1,8},{8,9},{9,16},{16,17},{17,24},{24,25},{25,0},{2,3},{3,1... | collective-permute-start | bytes 331784 | tf_op jit(solution)/shard_map/ppermute | solution.py:24
  46.5 24.4 %collective-permute-start.1 = (bf16[3,384,48]{2,1,0:T(8,128)(2,1)S(1)}, bf16[3,384,48]{2,1,0:T(8,128)(2,1)S(1)}, u32[]{:S(2)}, u32[]{:S(2)}) collective-permute-start(bf16[3,384,48]{2,1,0:T(8,128)(2,1)S(1)} %all_gather.11), channel_id=1, source_target_pairs={{0,25},{1,0},{8,1},{9,8},{16,9},{17,16},{24,17},{25,24},{2,27},{3,... | collective-permute-start | bytes 331784 | tf_op jit(solution)/shard_map/ppermute | solution.py:29
  60.6 11.7 %collective-permute-start.2 = (bf16[3,384,48]{2,1,0:T(8,128)(2,1)S(1)}, bf16[3,384,48]{2,1,0:T(8,128)(2,1)S(1)}, u32[]{:S(2)}, u32[]{:S(2)}) collective-permute-start(bf16[3,384,48]{2,1,0:T(8,128)(2,1)S(1)} %collective-permute-done), channel_id=1, source_target_pairs={{0,1},{1,8},{8,9},{9,16},{16,17},{17,24},{24,25},{25,0},{2,3},{3,1... | collective-permute-start | bytes 331784 | tf_op jit(solution)/shard_map/ppermute | solution.py:24
  63.8 10.0 %all-to-all-start = ((bf16[1,8,1,16,384]{4,1,2,0,3:T(8,128)(2,1)}), bf16[1,8,1,16,384]{4,1,2,0,3:T(8,128)(2,1)S(1)}, u32[]{:S(2)}, u32[]{:S(2)}) async-start(bf16[1,8,1,16,384]{4,1,2,0,3:T(8,128)(2,1)} %bitcast.310), calls=%async_computation | async-start | bytes 196608 | tf_op jit(solution)/shard_map/all_to_all | solution.py:94
  70.9 12.6 %collective-permute-start.3 = (bf16[3,384,48]{2,1,0:T(8,128)(2,1)S(1)}, bf16[3,384,48]{2,1,0:T(8,128)(2,1)S(1)}, u32[]{:S(2)}, u32[]{:S(2)}) collective-permute-start(bf16[3,384,48]{2,1,0:T(8,128)(2,1)S(1)} %collective-permute-done.1), channel_id=1, source_target_pairs={{0,25},{1,0},{8,1},{9,8},{16,9},{17,16},{24,17},{25,24},{2,27},{3,... | collective-permute-start | bytes 331784 | tf_op jit(solution)/shard_map/ppermute | solution.py:29
  72.4 11.2 %collective-permute-start.4 = (bf16[3,384,48]{2,1,0:T(8,128)(2,1)S(1)}, bf16[3,384,48]{2,1,0:T(8,128)(2,1)S(1)}, u32[]{:S(2)}, u32[]{:S(2)}) collective-permute-start(bf16[3,384,48]{2,1,0:T(8,128)(2,1)S(1)} %collective-permute-done.2), channel_id=1, source_target_pairs={{0,1},{1,8},{8,9},{9,16},{16,17},{17,24},{24,25},{25,0},{2,3},{3,1... | collective-permute-start | bytes 331784 | tf_op jit(solution)/shard_map/ppermute | solution.py:24
  73.8 41.7 %copy-start.1 = (bf16[1,8,1,16,384]{4,1,2,0,3:T(8,128)(2,1)}, bf16[1,8,1,16,384]{4,1,2,0,3:T(8,128)(2,1)S(1)}, u32[]{:S(2)}) copy-start(bf16[1,8,1,16,384]{4,1,2,0,3:T(8,128)(2,1)S(1)} %all-to-all-done) | copy-start | bytes 294916
  83.5 19.7 %collective-permute-start.5 = (bf16[3,384,48]{2,1,0:T(8,128)(2,1)S(1)}, bf16[3,384,48]{2,1,0:T(8,128)(2,1)S(1)}, u32[]{:S(2)}, u32[]{:S(2)}) collective-permute-start(bf16[3,384,48]{2,1,0:T(8,128)(2,1)S(1)} %collective-permute-done.3), channel_id=1, source_target_pairs={{0,25},{1,0},{8,1},{9,8},{16,9},{17,16},{24,17},{25,24},{2,27},{3,... | collective-permute-start | bytes 331784 | tf_op jit(solution)/shard_map/ppermute | solution.py:29
  83.5 22.9 %collective-permute-start.6 = (bf16[3,384,48]{2,1,0:T(8,128)(2,1)S(1)}, bf16[3,384,48]{2,1,0:T(8,128)(2,1)S(1)}, u32[]{:S(2)}, u32[]{:S(2)}) collective-permute-start(bf16[3,384,48]{2,1,0:T(8,128)(2,1)S(1)} %collective-permute-done.4), channel_id=1, source_target_pairs={{0,1},{1,8},{8,9},{9,16},{16,17},{17,24},{24,25},{25,0},{2,3},{3,1... | collective-permute-start | bytes 331784 | tf_op jit(solution)/shard_map/ppermute | solution.py:24
  114.1 22.0 %copy-start.40 = (f32[4,6,32]{2,1,0:T(8,128)}, f32[4,6,32]{2,1,0:T(8,128)S(1)}, u32[]{:S(2)}) copy-start(f32[4,6,32]{2,1,0:T(8,128)S(1)} %get-tuple-element.25) | copy-start | bytes 9220
  133.7 9.5 %copy-start.3 = (bf16[1,8,1,16,384]{4,1,2,0,3:T(8,128)(2,1)}, bf16[1,8,1,16,384]{4,1,2,0,3:T(8,128)(2,1)S(1)}, u32[]{:S(2)}) copy-start(bf16[1,8,1,16,384]{4,1,2,0,3:T(8,128)(2,1)S(1)} %all_to_all.133) | copy-start | bytes 294916
  204.8 16.1 %copy-start.10 = (f32[8,4,6,4]{3,2,1,0:T(8,128)S(1)}, f32[8,4,6,4]{3,2,1,0:T(8,128)}, u32[]{:S(2)}) copy-start(f32[8,4,6,4]{3,2,1,0:T(8,128)} %copy-done.9) | copy-start | bytes 9220
  204.8 27.4 %copy-start.6 = (f32[8,4,6,4,4]{3,4,2,1,0:T(4,128)S(1)}, f32[8,4,6,4,4]{3,4,2,1,0:T(4,128)}, u32[]{:S(2)}) copy-start(f32[8,4,6,4,4]{3,4,2,1,0:T(4,128)} %copy-done.5) | copy-start | bytes 36868
  216.7 9.8 %all-to-all-start.6 = ((bf16[1,8,1,16,384]{4,1,2,0,3:T(8,128)(2,1)}), bf16[1,8,1,16,384]{4,1,2,0,3:T(8,128)(2,1)}, u32[]{:S(2)}, u32[]{:S(2)}) async-start(bf16[1,8,1,16,384]{4,1,2,0,3:T(8,128)(2,1)} %all_to_all.112), calls=%async_computation.6 | async-start | bytes 196608 | tf_op jit(solution)/shard_map/all_to_all | solution.py:102
  245.5 17.7 %copy-start.41 = (f32[4,6,32]{2,1,0:T(8,128)S(1)}, f32[4,6,32]{2,1,0:T(8,128)}, u32[]{:S(2)}) copy-start(f32[4,6,32]{2,1,0:T(8,128)} %copy-done.40) | copy-start | bytes 9220
  245.5 17.7 %copy-start.32 = (f32[32,4,6]{0,1,2:T(4,128)S(1)}, f32[32,4,6]{0,1,2:T(4,128)}, u32[]{:S(2)}) copy-start(f32[32,4,6]{0,1,2:T(4,128)} %copy-done.31) | copy-start | bytes 9220
  246.3 21.5 %copy-start.8 = (f32[4,6,32,32]{2,3,1,0:T(8,128)S(1)}, f32[4,6,32,32]{2,3,1,0:T(8,128)}, u32[]{:S(2)}) copy-start(f32[4,6,32,32]{2,3,1,0:T(8,128)} %copy-done.7) | copy-start | bytes 294916
  246.6 21.5 %copy-start.12 = (bf16[32,4,6,64]{3,2,0,1:T(8,128)(2,1)S(1)}, bf16[32,4,6,64]{3,2,0,1:T(8,128)(2,1)}, u32[]{:S(2)}) copy-start(bf16[32,4,6,64]{3,2,0,1:T(8,128)(2,1)} %copy-done.11) | copy-start | bytes 294916
  248.3 20.1 %copy-start.18 = (bf16[32,4,6,64]{3,2,0,1:T(8,128)(2,1)S(1)}, bf16[32,4,6,64]{3,2,0,1:T(8,128)(2,1)}, u32[]{:S(2)}) copy-start(bf16[32,4,6,64]{3,2,0,1:T(8,128)(2,1)} %copy-done.17) | copy-start | bytes 294916
  250.0 9.8 %all-to-all-start.7 = ((bf16[1,8,4,4,384]{4,1,3,0,2:T(8,128)(2,1)}), bf16[1,8,4,4,384]{4,1,3,0,2:T(8,128)(2,1)}, u32[]{:S(2)}, u32[]{:S(2)}) async-start(bf16[1,8,4,4,384]{4,1,3,0,2:T(8,128)(2,1)} %fusion.88), calls=%async_computation.7 | async-start | bytes 196608 | tf_op jit(solution)/shard_map/all_to_all | solution.py:106
  259.8 7.6 %all-to-all-start.8 = ((bf16[1,8,1,16,384]{4,1,2,0,3:T(8,128)(2,1)}), bf16[1,8,1,16,384]{4,1,2,0,3:T(8,128)(2,1)S(1)}, u32[]{:S(2)}, u32[]{:S(2)}) async-start(bf16[1,8,1,16,384]{4,1,2,0,3:T(8,128)(2,1)} %bitcast.68), calls=%async_computation.8 | async-start | bytes 196608 | tf_op jit(solution)/shard_map/all_to_all | solution.py:94
  (33 other events, 98.4 us)
Sparse Core Ops, SparseCore 0:
  30.4 40.1 all-gather.1
